TPU v7x, 256 devices: a whole 4x4x8 slice. The times are simulated.
256 devices in a mesh: seq: 64 (over z_hi, y, x, core), tp: 4 (over z_lo).
Axes of the slice: x: 4, y: 4, z: 8 (z_hi: 2, z_lo: 4; z = z_hi * 4 + z_lo), core: 2. Of those that a mesh axis runs over, the one named last changes fastest.
Arguments:
- residual: bfloat16 [32768, 2048], P('seq', 'tp'), may hold values from -6 to 6
- norm_gain: float32 [2048], replicated, may hold values from 0.3 to 3
- query_weight: bfloat16 [2048, 1024], P(None, 'tp'), as said below
- key_weight: bfloat16 [2048, 1024], P(None, 'tp'), as said below
- value_weight: bfloat16 [2048, 1024], P(None, 'tp'), may hold values from -0.375 to 0.375
- out_weight: bfloat16 [1024, 2048], P('tp'), may hold values from -0.1875 to 0.1875
- segment_start: int32 [32768], P('seq'), may hold values from 0 to 32640, as said below
- token_valid: int32 [32768], P('seq'), may hold values from 0 to 1, as said below
- page_slot: int32 [256], P('seq'), may hold values from 4 to 511, as said below
Outputs:
- hidden: bfloat16 [32768, 2048], P('seq', 'tp')
- cache: bfloat16 [512, 128, 2048], P('seq', None, 'tp')
Inputs may be any that keep to these rules, and one draw needn't show every extreme that they name: `segment_start`: prompts start at multiples of 128 and are contiguous; each holds at most 8192 tokens and one holds exactly 8192. `token_valid`: zeros form a tail of the last page of a prompt; the first token of every prompt is 1. No two pages share a cache page; page_slot // 8 is the device that holds the page's tokens, or the next device when that one holds tokens of the same prompt. `query_weight`: independent entries whose scale falls as the inverse square root of 2048. `key_weight`: independent entries whose scale falls as the inverse square root of 2048.
All inputs are finite; a program needn't handle non-finite values.
Results may differ from a plain program's by a relative error of at most 0.02.
The roundings to bfloat16 on the way count: a program that leaves them out, or rounds other values in their place, can miss the bound.
Values may be sent and summed in bfloat16 or wider, within the bound.
No kernel may reach another device: no remote copies, remote signals or barrier semaphores. Data moves between devices by JAX's collectives and lax.ppermute only.
A program may use at most 128 MiB of HBM per device.

v0:
```python
import jax
import jax.numpy as jnp
from jax import lax
from jax.sharding import PartitionSpec as P

HD = 64
PAGE = 128
SPAN = 16
THETA = 130000.0
EPS = 1e-05


def passed_along(x, axis, by):
    count = lax.axis_size(axis)
    pairs = [(i, i + by) for i in range(count) if 0 <= i + by < count]
    return lax.ppermute(x, axis, pairs)


def rotate(inputs, positions):
    half_dim = inputs.shape[-1] // 2
    frequency = THETA ** (-2.0 * jnp.arange(half_dim, dtype=jnp.float32) / inputs.shape[-1])
    angles = positions.astype(jnp.float32)[:, None] * frequency[None, :]
    cosine = jnp.cos(angles)[:, None, :]
    sine_part = jnp.sin(angles)[:, None, :]
    front_half = inputs[..., :half_dim]
    back_half = inputs[..., half_dim:]
    return jnp.concatenate(
        [front_half * cosine - back_half * sine_part, back_half * cosine + front_half * sine_part],
        axis=-1,
    )


def body(
    residual,
    norm_gain,
    query_weight,
    key_weight,
    value_weight,
    out_weight,
    segment_start,
    token_valid,
    page_slot,
):
    row_count = residual.shape[0]
    local_heads = query_weight.shape[1] // HD
    gathered = lax.all_gather(residual, "tp", axis=1, tiled=True)
    widened = gathered.astype(jnp.float32)
    mean_sq = jnp.mean(widened * widened, axis=1, keepdims=True)
    normed = (widened * lax.rsqrt(mean_sq + EPS) * norm_gain[None, :]).astype(jnp.bfloat16)
    seq_rank = lax.axis_index("seq")
    first_row = seq_rank * row_count
    places = first_row + jnp.arange(row_count, dtype=jnp.int32)
    offsets = places - segment_start
    queries = jnp.dot(normed, query_weight, preferred_element_type=jnp.float32).reshape(
        row_count, local_heads, HD
    )
    queries = rotate(queries, offsets).astype(jnp.bfloat16)
    key_rot = jnp.dot(normed, key_weight, preferred_element_type=jnp.float32).reshape(
        row_count, local_heads, HD
    )
    key_rot = rotate(key_rot, offsets).astype(jnp.bfloat16)
    values = (
        jnp.dot(normed, value_weight, preferred_element_type=jnp.float32)
        .reshape(row_count, local_heads, HD)
        .astype(jnp.bfloat16)
    )
    packed = jnp.concatenate([key_rot[:, :, None, :], values[:, :, None, :]], axis=2).reshape(
        row_count, local_heads * 2 * HD
    )
    packed = jnp.where(token_valid[:, None] > 0, packed, jnp.zeros_like(packed))
    score_scale = HD ** (-0.5)
    out_cols = lax.all_to_all(out_weight, "tp", 1, 0, tiled=True)
    prev_slot = passed_along(page_slot, "seq", 1)

    def attend_block(running, incoming, allowed):
        row_max, norm_sum, weighted = running
        key_value = incoming.reshape(incoming.shape[0], local_heads, 2, HD)
        scores = (
            jnp.einsum(
                "qhd,khd->hqk", queries, key_value[:, :, 0, :], preferred_element_type=jnp.float32
            )
            * score_scale
        )
        block_max = jnp.max(jnp.where(allowed[None], scores, -1e30), axis=2)
        new_max = jnp.maximum(row_max, block_max)
        weights = jnp.where(allowed[None], jnp.exp(scores - new_max[:, :, None]), 0.0)
        shrink = jnp.exp(row_max - new_max)
        norm_sum = norm_sum * shrink + jnp.sum(weights, axis=2)
        update = jnp.einsum(
            "hqk,khd->qhd",
            weights.astype(jnp.bfloat16),
            key_value[:, :, 1, :],
            preferred_element_type=jnp.float32,
        )
        weighted = weighted * jnp.transpose(shrink)[:, :, None] + update
        return (new_max, norm_sum, weighted)

    local_pos = jnp.arange(row_count, dtype=jnp.int32)
    own_allowed = (
        ((first_row + local_pos)[None, :] >= segment_start[:, None])
        & (local_pos[None, :] <= local_pos[:, None])
        & (token_valid[None, :] > 0)
    )
    initial = (
        jnp.full((local_heads, row_count), -1e30, jnp.float32),
        jnp.zeros((local_heads, row_count), jnp.float32),
        jnp.zeros((row_count, local_heads, HD), jnp.float32),
    )
    carried = attend_block(initial, packed, own_allowed)

    def remote_absorb(running, incoming, step):
        key_places = first_row - step * row_count + local_pos
        allowed = key_places[None, :] >= segment_start[:, None]
        return attend_block(running, incoming, allowed)

    prev_block = passed_along(packed, "seq", 1)
    carried = remote_absorb(carried, prev_block, 1)
    reach_dev = min(SPAN, lax.axis_size("seq") // 2)

    def advance(step_index, carry_in):
        moving, running = carry_in
        moving = passed_along(moving, "seq", 1)
        running = remote_absorb(running, moving, step_index)
        return (moving, running)

    _, carried = lax.fori_loop(2, reach_dev + 1, advance, (prev_block, carried))
    row_max, norm_sum, weighted = carried
    attended = (
        (weighted / jnp.transpose(norm_sum)[:, :, None])
        .astype(jnp.bfloat16)
        .reshape(row_count, local_heads * HD)
    )
    tiles = page_slot.shape[0]
    slot_count = 2 * tiles
    base_slot = seq_rank * slot_count
    has_prev = seq_rank > 0
    cand_slot = jnp.concatenate([page_slot, jnp.where(has_prev, prev_slot, -1)]) - base_slot
    cand_pages = jnp.concatenate(
        [packed.reshape(tiles, PAGE, -1), prev_block.reshape(tiles, PAGE, -1)], axis=0
    )
    match = cand_slot[None, :] == jnp.arange(slot_count, dtype=jnp.int32)[:, None]
    pick = jnp.argmax(match.astype(jnp.int32), axis=1)
    found = jnp.any(match, axis=1)
    cache_pages = jnp.where(found[:, None, None], cand_pages[pick], jnp.zeros_like(cand_pages[:1]))
    attended_all = lax.all_gather(attended, "tp", axis=1, tiled=True)
    projected = jnp.dot(attended_all, out_cols, preferred_element_type=jnp.float32)
    hidden = (residual.astype(jnp.float32) + projected).astype(jnp.bfloat16)
    return (hidden, cache_pages)


def solution(mesh):
    return jax.shard_map(
        body,
        mesh=mesh,
        in_specs=(
            P("seq", "tp"),
            P(),
            P(None, "tp"),
            P(None, "tp"),
            P(None, "tp"),
            P("tp", None),
            P("seq"),
            P("seq"),
            P("seq"),
        ),
        out_specs=(P("seq", "tp"), P("seq", None, "tp")),
        check_vma=False,
    )
```

profile of v0, /device:TPU:1, one launch (start us, length us, event | category | flops | bytes accessed | tf_op | source)
XLA Modules:
  0.0 500.1 jit_solution(5178662731228044125)
XLA Ops:
  8.0 2.3 copy.46
  10.2 6.4 %all-to-all-start = ((bf16[256,4,512]{0,2,1:T(8,128)(2,1)}), bf16[256,4,512]{0,2,1:T(8,128)(2,1)S(1)}, u32[]{:S(2)}, u32[]{:S(2)}) async-start(bf16[256,4,512]{0,2,1:T(8,128)(2,1)} %bitcast.17), calls=%async_computation | async-start | bytes 2097152 | tf_op jit(solution)/shard_map/all_to_all | solution.py:72
  16.7 4.0 collective-permute-start.2
  21.0 1.2 fusion.47
  22.2 50.8 %all-gather.3.cloned.1.call-done = bf16[512,2048]{1,0:T(8,128)(2,1)} async-done(((bf16[512,512]{1,0:T(8,128)(2,1)}), bf16[512,2048]{1,0:T(8,128)(2,1)}) %all-gather.3.cloned.1.call-update) | async-done | bytes 2097168 | tf_op jit(solution)/shard_map/all_gather | solution.py:46
  73.0 2.2 fusion.17
  75.3 2.5 fusion.64
  77.8 2.3 fusion.61
  83.7 5.1 %collective-permute-start.1 = (bf16[512,512]{0,1:T(8,128)(2,1)}, bf16[512,512]{0,1:T(8,128)(2,1)S(1)}, u32[]{:S(2)}, u32[]{:S(2)}) collective-permute-start(bf16[512,512]{0,1:T(8,128)(2,1)} %bitcast_select_fusion), channel_id=1, source_target_pairs={{0,4},{4,8},{8,12},{12,16},{16,20},{20,24},{24,28},{28,32},{32,36}... | collective-permute-start | bytes 1572872 | tf_op jit(solution)/shard_map/ppermute | solution.py:16
  89.7 2.0 select_reduce_fusion.2
  91.8 3.2 collective-permute-done.1
  95.0 2.1 select_reduce_fusion.1
  100.1 1.9 fusion.37
  102.8 220.3 %while.20 = (s32[]{:T(128)}, bf16[512,512]{0,1:T(8,128)(2,1)}, f32[4,512]{1,0:T(4,128)S(1)}, f32[4,512]{1,0:T(4,128)S(1)}, f32[512,4,64]{0,2,1:T(8,128)}, /*inde...) while((s32[]{:T(128)}, bf16[512,512]{0,1:T(8,128)(2,1)}, ...), condition=%wide.region_8.9_spmd.clone, body=%wide.region_5.8_spmd.clone.sunk | while | flops 280500736 | bytes 22943988 | solution.py:126
  102.8 4.3 collective-permute-start
  107.3 6.2 %collective-permute-done = bf16[512,512]{0,1:T(8,128)(2,1)S(1)} collective-permute-done((bf16[512,512]{0,1:T(8,128)(2,1)}, bf16[512,512]{0,1:T(8,128)(2,1)S(1)}, u32[]{:S(2)}, u32[]{:S(2)}) %collective-permute-start) | collective-permute-done | bytes 524320 | tf_op jit(solution)/shard_map/while/body/eval_jaxpr/ppermute | solution.py:16
  115.4 1.1 fusion.82
  117.5 4.3 collective-permute-start
  122.0 6.2 %collective-permute-done = bf16[512,512]{0,1:T(8,128)(2,1)S(1)} collective-permute-done((bf16[512,512]{0,1:T(8,128)(2,1)}, bf16[512,512]{0,1:T(8,128)(2,1)S(1)}, u32[]{:S(2)}, u32[]{:S(2)}) %collective-permute-start) | collective-permute-done | bytes 524320 | tf_op jit(solution)/shard_map/while/body/eval_jaxpr/ppermute | solution.py:16
  130.0 1.1 fusion.82
  132.1 4.3 collective-permute-start
  136.7 6.2 %collective-permute-done = bf16[512,512]{0,1:T(8,128)(2,1)S(1)} collective-permute-done((bf16[512,512]{0,1:T(8,128)(2,1)}, bf16[512,512]{0,1:T(8,128)(2,1)S(1)}, u32[]{:S(2)}, u32[]{:S(2)}) %collective-permute-start) | collective-permute-done | bytes 524320 | tf_op jit(solution)/shard_map/while/body/eval_jaxpr/ppermute | solution.py:16
  144.7 1.1 fusion.82
  146.8 4.3 collective-permute-start
  151.4 6.2 %collective-permute-done = bf16[512,512]{0,1:T(8,128)(2,1)S(1)} collective-permute-done((bf16[512,512]{0,1:T(8,128)(2,1)}, bf16[512,512]{0,1:T(8,128)(2,1)S(1)}, u32[]{:S(2)}, u32[]{:S(2)}) %collective-permute-start) | collective-permute-done | bytes 524320 | tf_op jit(solution)/shard_map/while/body/eval_jaxpr/ppermute | solution.py:16
  159.4 1.1 fusion.82
  161.5 4.3 collective-permute-start
  166.0 6.2 %collective-permute-done = bf16[512,512]{0,1:T(8,128)(2,1)S(1)} collective-permute-done((bf16[512,512]{0,1:T(8,128)(2,1)}, bf16[512,512]{0,1:T(8,128)(2,1)S(1)}, u32[]{:S(2)}, u32[]{:S(2)}) %collective-permute-start) | collective-permute-done | bytes 524320 | tf_op jit(solution)/shard_map/while/body/eval_jaxpr/ppermute | solution.py:16
  174.1 1.1 fusion.82
  176.2 4.3 collective-permute-start
  180.7 6.2 %collective-permute-done = bf16[512,512]{0,1:T(8,128)(2,1)S(1)} collective-permute-done((bf16[512,512]{0,1:T(8,128)(2,1)}, bf16[512,512]{0,1:T(8,128)(2,1)S(1)}, u32[]{:S(2)}, u32[]{:S(2)}) %collective-permute-start) | collective-permute-done | bytes 524320 | tf_op jit(solution)/shard_map/while/body/eval_jaxpr/ppermute | solution.py:16
  188.8 1.1 fusion.82
  190.9 4.3 collective-permute-start
  195.4 6.2 %collective-permute-done = bf16[512,512]{0,1:T(8,128)(2,1)S(1)} collective-permute-done((bf16[512,512]{0,1:T(8,128)(2,1)}, bf16[512,512]{0,1:T(8,128)(2,1)S(1)}, u32[]{:S(2)}, u32[]{:S(2)}) %collective-permute-start) | collective-permute-done | bytes 524320 | tf_op jit(solution)/shard_map/while/body/eval_jaxpr/ppermute | solution.py:16
  203.5 1.1 fusion.82
  205.6 4.3 collective-permute-start
  210.1 6.2 %collective-permute-done = bf16[512,512]{0,1:T(8,128)(2,1)S(1)} collective-permute-done((bf16[512,512]{0,1:T(8,128)(2,1)}, bf16[512,512]{0,1:T(8,128)(2,1)S(1)}, u32[]{:S(2)}, u32[]{:S(2)}) %collective-permute-start) | collective-permute-done | bytes 524320 | tf_op jit(solution)/shard_map/while/body/eval_jaxpr/ppermute | solution.py:16
  218.2 1.1 fusion.82
  220.3 4.3 collective-permute-start
  224.8 6.2 %collective-permute-done = bf16[512,512]{0,1:T(8,128)(2,1)S(1)} collective-permute-done((bf16[512,512]{0,1:T(8,128)(2,1)}, bf16[512,512]{0,1:T(8,128)(2,1)S(1)}, u32[]{:S(2)}, u32[]{:S(2)}) %collective-permute-start) | collective-permute-done | bytes 524320 | tf_op jit(solution)/shard_map/while/body/eval_jaxpr/ppermute | solution.py:16
  232.8 1.1 fusion.82
  234.9 4.3 collective-permute-start
  239.5 6.2 %collective-permute-done = bf16[512,512]{0,1:T(8,128)(2,1)S(1)} collective-permute-done((bf16[512,512]{0,1:T(8,128)(2,1)}, bf16[512,512]{0,1:T(8,128)(2,1)S(1)}, u32[]{:S(2)}, u32[]{:S(2)}) %collective-permute-start) | collective-permute-done | bytes 524320 | tf_op jit(solution)/shard_map/while/body/eval_jaxpr/ppermute | solution.py:16
  247.5 1.1 fusion.82
  249.6 4.3 collective-permute-start
  254.2 6.2 %collective-permute-done = bf16[512,512]{0,1:T(8,128)(2,1)S(1)} collective-permute-done((bf16[512,512]{0,1:T(8,128)(2,1)}, bf16[512,512]{0,1:T(8,128)(2,1)S(1)}, u32[]{:S(2)}, u32[]{:S(2)}) %collective-permute-start) | collective-permute-done | bytes 524320 | tf_op jit(solution)/shard_map/while/body/eval_jaxpr/ppermute | solution.py:16
  262.2 1.1 fusion.82
  264.3 4.3 collective-permute-start
  268.8 6.2 %collective-permute-done = bf16[512,512]{0,1:T(8,128)(2,1)S(1)} collective-permute-done((bf16[512,512]{0,1:T(8,128)(2,1)}, bf16[512,512]{0,1:T(8,128)(2,1)S(1)}, u32[]{:S(2)}, u32[]{:S(2)}) %collective-permute-start) | collective-permute-done | bytes 524320 | tf_op jit(solution)/shard_map/while/body/eval_jaxpr/ppermute | solution.py:16
  276.9 1.1 fusion.82
  279.0 4.3 collective-permute-start
  283.5 6.2 %collective-permute-done = bf16[512,512]{0,1:T(8,128)(2,1)S(1)} collective-permute-done((bf16[512,512]{0,1:T(8,128)(2,1)}, bf16[512,512]{0,1:T(8,128)(2,1)S(1)}, u32[]{:S(2)}, u32[]{:S(2)}) %collective-permute-start) | collective-permute-done | bytes 524320 | tf_op jit(solution)/shard_map/while/body/eval_jaxpr/ppermute | solution.py:16
  291.6 1.1 fusion.82
  293.7 4.3 collective-permute-start
  298.2 6.2 %collective-permute-done = bf16[512,512]{0,1:T(8,128)(2,1)S(1)} collective-permute-done((bf16[512,512]{0,1:T(8,128)(2,1)}, bf16[512,512]{0,1:T(8,128)(2,1)S(1)}, u32[]{:S(2)}, u32[]{:S(2)}) %collective-permute-start) | collective-permute-done | bytes 524320 | tf_op jit(solution)/shard_map/while/body/eval_jaxpr/ppermute | solution.py:16
  306.3 1.1 fusion.82
  308.4 4.3 collective-permute-start
  312.9 6.2 %collective-permute-done = bf16[512,512]{0,1:T(8,128)(2,1)S(1)} collective-permute-done((bf16[512,512]{0,1:T(8,128)(2,1)}, bf16[512,512]{0,1:T(8,128)(2,1)S(1)}, u32[]{:S(2)}, u32[]{:S(2)}) %collective-permute-start) | collective-permute-done | bytes 524320 | tf_op jit(solution)/shard_map/while/body/eval_jaxpr/ppermute | solution.py:16
  321.0 1.1 fusion.82
  323.1 1.8 divide_convert_fusion
  326.5 1.3 copy.47
  329.4 1.3 copy.50
  332.5 157.5 %all-gather.5.cloned.1.call-done = bf16[512,1024]{0,1:T(8,128)(2,1)} async-done(((bf16[512,256]{0,1:T(8,128)(2,1)}), bf16[512,1024]{0,1:T(8,128)(2,1)}) %all-gather.5.cloned.1.call-update) | async-done | bytes 1048592 | tf_op jit(solution)/shard_map/all_gather | solution.py:145
  490.0 3.2 fusion.30
  (240 shorter events, 59.8 us)
Async XLA Ops:
  7.2 68.1 %copy-start = (bf16[2048,256]{1,0:T(8,128)(2,1)S(1)}, bf16[2048,256]{1,0:T(8,128)(2,1)}, u32[]{:S(2)}) copy-start(bf16[2048,256]{1,0:T(8,128)(2,1)} %param.14) | copy-start | bytes 3145732
  7.2 9.5 %copy-start.10 = (s32[4]{0:T(128)S(1)}, s32[4]{0:T(128)}, u32[]{:S(2)}) copy-start(s32[4]{0:T(128)} %param.19) | copy-start | bytes 52
  7.2 13.5 %copy-start.9 = (s32[512]{0:T(512)S(1)}, s32[512]{0:T(512)}, u32[]{:S(2)}) copy-start(s32[512]{0:T(512)} %param.18) | copy-start | bytes 6148
  7.2 13.5 %copy-start.8 = (s32[512]{0:T(512)S(1)}, s32[512]{0:T(512)}, u32[]{:S(2)}) copy-start(s32[512]{0:T(512)} %param.17) | copy-start | bytes 6148
  7.2 68.1 %copy-start.12 = (f32[2048]{0:T(1024)S(1)}, f32[2048]{0:T(1024)}, u32[]{:S(2)}) copy-start(f32[2048]{0:T(1024)} %param.12) | copy-start | bytes 24580
  7.2 65.8 %all-gather.3.cloned.1.call-start = ((), (), s32[]{:S(2)}) async-start(), calls=%async_computation.1 | async-start | bytes 2621440 | tf_op jit(solution)/shard_map/all_gather | solution.py:46
  10.2 316.2 %all-to-all-start = ((bf16[256,4,512]{0,2,1:T(8,128)(2,1)}), bf16[256,4,512]{0,2,1:T(8,128)(2,1)S(1)}, u32[]{:S(2)}, u32[]{:S(2)}) async-start(bf16[256,4,512]{0,2,1:T(8,128)(2,1)} %bitcast.17), calls=%async_computation | async-start | bytes 2097152 | tf_op jit(solution)/shard_map/all_to_all | solution.py:72
  16.7 473.4 %all-gather.5.cloned.1.call-start = ((), (), s32[]{:S(2)}) async-start(), calls=%async_computation.2 | async-start | bytes 1310720 | tf_op jit(solution)/shard_map/all_gather | solution.py:145
  16.7 308.2 %collective-permute-start.2 = (s32[4]{0:T(128)S(1)}, s32[4]{0:T(128)}, u32[]{:S(2)}, u32[]{:S(2)}) collective-permute-start(s32[4]{0:T(128)S(1)} %copy-done.10), channel_id=1, source_target_pairs={{0,4},{4,8},{8,12},{12,16},{16,20},{20,24},{24,28},{28,32},{32,36}... | collective-permute-start | bytes 56 | tf_op jit(solution)/shard_map/ppermute | solution.py:16
  73.0 4.8 copy-start.1
  77.8 3.1 copy-start.11
  83.7 11.3 %collective-permute-start.1 = (bf16[512,512]{0,1:T(8,128)(2,1)}, bf16[512,512]{0,1:T(8,128)(2,1)S(1)}, u32[]{:S(2)}, u32[]{:S(2)}) collective-permute-start(bf16[512,512]{0,1:T(8,128)(2,1)} %bitcast_select_fusion), channel_id=1, source_target_pairs={{0,4},{4,8},{8,12},{12,16},{16,20},{20,24},{24,28},{28,32},{32,36}... | collective-permute-start | bytes 1572872 | tf_op jit(solution)/shard_map/ppermute | solution.py:16
  89.7 7.5 %copy-start.4 = (pred[512,512]{0,1:T(8,128)(4,1)S(1)}, pred[512,512]{0,1:T(8,128)(4,1)}, u32[]{:S(2)}) copy-start(pred[512,512]{0,1:T(8,128)(4,1)} %get-tuple-element.213) | copy-start | bytes 786436
  95.0 7.0 %copy-start.2 = (bf16[512,512]{0,1:T(8,128)(2,1)}, bf16[512,512]{0,1:T(8,128)(2,1)S(1)}, u32[]{:S(2)}) copy-start(bf16[512,512]{0,1:T(8,128)(2,1)S(1)} %collective-permute-done.1) | copy-start | bytes 1572868
  95.0 3.1 copy-start.7
  98.1 1.1 copy-start.3
  102.8 10.7 %collective-permute-start = (bf16[512,512]{0,1:T(8,128)(2,1)}, bf16[512,512]{0,1:T(8,128)(2,1)S(1)}, u32[]{:S(2)}, u32[]{:S(2)}) collective-permute-start(bf16[512,512]{0,1:T(8,128)(2,1)} %get-tuple-element.290), channel_id=1, source_target_pairs={{0,4},{4,8},{8,12},{12,16},{16,20},{20,24},{24,28},{28,32},{32,36}... | collective-permute-start | bytes 1572872 | tf_op jit(solution)/shard_map/while/body/eval_jaxpr/ppermute | solution.py:16
  113.5 1.9 copy-start.5
  116.5 1.0 copy-start.6
  117.5 10.7 %collective-permute-start = (bf16[512,512]{0,1:T(8,128)(2,1)}, bf16[512,512]{0,1:T(8,128)(2,1)S(1)}, u32[]{:S(2)}, u32[]{:S(2)}) collective-permute-start(bf16[512,512]{0,1:T(8,128)(2,1)} %get-tuple-element.290), channel_id=1, source_target_pairs={{0,4},{4,8},{8,12},{12,16},{16,20},{20,24},{24,28},{28,32},{32,36}... | collective-permute-start | bytes 1572872 | tf_op jit(solution)/shard_map/while/body/eval_jaxpr/ppermute | solution.py:16
  128.2 1.9 copy-start.5
  131.2 1.0 copy-start.6
  132.1 10.7 %collective-permute-start = (bf16[512,512]{0,1:T(8,128)(2,1)}, bf16[512,512]{0,1:T(8,128)(2,1)S(1)}, u32[]{:S(2)}, u32[]{:S(2)}) collective-permute-start(bf16[512,512]{0,1:T(8,128)(2,1)} %get-tuple-element.290), channel_id=1, source_target_pairs={{0,4},{4,8},{8,12},{12,16},{16,20},{20,24},{24,28},{28,32},{32,36}... | collective-permute-start | bytes 1572872 | tf_op jit(solution)/shard_map/while/body/eval_jaxpr/ppermute | solution.py:16
  142.8 1.9 copy-start.5
  145.9 1.0 copy-start.6
  146.8 10.7 %collective-permute-start = (bf16[512,512]{0,1:T(8,128)(2,1)}, bf16[512,512]{0,1:T(8,128)(2,1)S(1)}, u32[]{:S(2)}, u32[]{:S(2)}) collective-permute-start(bf16[512,512]{0,1:T(8,128)(2,1)} %get-tuple-element.290), channel_id=1, source_target_pairs={{0,4},{4,8},{8,12},{12,16},{16,20},{20,24},{24,28},{28,32},{32,36}... | collective-permute-start | bytes 1572872 | tf_op jit(solution)/shard_map/while/body/eval_jaxpr/ppermute | solution.py:16
  157.5 1.9 copy-start.5
  160.5 1.0 copy-start.6
  161.5 10.7 %collective-permute-start = (bf16[512,512]{0,1:T(8,128)(2,1)}, bf16[512,512]{0,1:T(8,128)(2,1)S(1)}, u32[]{:S(2)}, u32[]{:S(2)}) collective-permute-start(bf16[512,512]{0,1:T(8,128)(2,1)} %get-tuple-element.290), channel_id=1, source_target_pairs={{0,4},{4,8},{8,12},{12,16},{16,20},{20,24},{24,28},{28,32},{32,36}... | collective-permute-start | bytes 1572872 | tf_op jit(solution)/shard_map/while/body/eval_jaxpr/ppermute | solution.py:16
  172.2 1.9 copy-start.5
  175.2 1.0 copy-start.6
  176.2 10.7 %collective-permute-start = (bf16[512,512]{0,1:T(8,128)(2,1)}, bf16[512,512]{0,1:T(8,128)(2,1)S(1)}, u32[]{:S(2)}, u32[]{:S(2)}) collective-permute-start(bf16[512,512]{0,1:T(8,128)(2,1)} %get-tuple-element.290), channel_id=1, source_target_pairs={{0,4},{4,8},{8,12},{12,16},{16,20},{20,24},{24,28},{28,32},{32,36}... | collective-permute-start | bytes 1572872 | tf_op jit(solution)/shard_map/while/body/eval_jaxpr/ppermute | solution.py:16
  186.9 1.9 copy-start.5
  189.9 1.0 copy-start.6
  190.9 10.7 %collective-permute-start = (bf16[512,512]{0,1:T(8,128)(2,1)}, bf16[512,512]{0,1:T(8,128)(2,1)S(1)}, u32[]{:S(2)}, u32[]{:S(2)}) collective-permute-start(bf16[512,512]{0,1:T(8,128)(2,1)} %get-tuple-element.290), channel_id=1, source_target_pairs={{0,4},{4,8},{8,12},{12,16},{16,20},{20,24},{24,28},{28,32},{32,36}... | collective-permute-start | bytes 1572872 | tf_op jit(solution)/shard_map/while/body/eval_jaxpr/ppermute | solution.py:16
  201.6 1.9 copy-start.5
  204.6 1.0 copy-start.6
  205.6 10.7 %collective-permute-start = (bf16[512,512]{0,1:T(8,128)(2,1)}, bf16[512,512]{0,1:T(8,128)(2,1)S(1)}, u32[]{:S(2)}, u32[]{:S(2)}) collective-permute-start(bf16[512,512]{0,1:T(8,128)(2,1)} %get-tuple-element.290), channel_id=1, source_target_pairs={{0,4},{4,8},{8,12},{12,16},{16,20},{20,24},{24,28},{28,32},{32,36}... | collective-permute-start | bytes 1572872 | tf_op jit(solution)/shard_map/while/body/eval_jaxpr/ppermute | solution.py:16
  216.3 1.9 copy-start.5
  219.3 1.0 copy-start.6
  220.3 10.7 %collective-permute-start = (bf16[512,512]{0,1:T(8,128)(2,1)}, bf16[512,512]{0,1:T(8,128)(2,1)S(1)}, u32[]{:S(2)}, u32[]{:S(2)}) collective-permute-start(bf16[512,512]{0,1:T(8,128)(2,1)} %get-tuple-element.290), channel_id=1, source_target_pairs={{0,4},{4,8},{8,12},{12,16},{16,20},{20,24},{24,28},{28,32},{32,36}... | collective-permute-start | bytes 1572872 | tf_op jit(solution)/shard_map/while/body/eval_jaxpr/ppermute | solution.py:16
  231.0 1.9 copy-start.5
  234.0 1.0 copy-start.6
  234.9 10.7 %collective-permute-start = (bf16[512,512]{0,1:T(8,128)(2,1)}, bf16[512,512]{0,1:T(8,128)(2,1)S(1)}, u32[]{:S(2)}, u32[]{:S(2)}) collective-permute-start(bf16[512,512]{0,1:T(8,128)(2,1)} %get-tuple-element.290), channel_id=1, source_target_pairs={{0,4},{4,8},{8,12},{12,16},{16,20},{20,24},{24,28},{28,32},{32,36}... | collective-permute-start | bytes 1572872 | tf_op jit(solution)/shard_map/while/body/eval_jaxpr/ppermute | solution.py:16
  245.6 1.9 copy-start.5
  248.7 1.0 copy-start.6
  249.6 10.7 %collective-permute-start = (bf16[512,512]{0,1:T(8,128)(2,1)}, bf16[512,512]{0,1:T(8,128)(2,1)S(1)}, u32[]{:S(2)}, u32[]{:S(2)}) collective-permute-start(bf16[512,512]{0,1:T(8,128)(2,1)} %get-tuple-element.290), channel_id=1, source_target_pairs={{0,4},{4,8},{8,12},{12,16},{16,20},{20,24},{24,28},{28,32},{32,36}... | collective-permute-start | bytes 1572872 | tf_op jit(solution)/shard_map/while/body/eval_jaxpr/ppermute | solution.py:16
  260.3 1.9 copy-start.5
  263.3 1.0 copy-start.6
  264.3 10.7 %collective-permute-start = (bf16[512,512]{0,1:T(8,128)(2,1)}, bf16[512,512]{0,1:T(8,128)(2,1)S(1)}, u32[]{:S(2)}, u32[]{:S(2)}) collective-permute-start(bf16[512,512]{0,1:T(8,128)(2,1)} %get-tuple-element.290), channel_id=1, source_target_pairs={{0,4},{4,8},{8,12},{12,16},{16,20},{20,24},{24,28},{28,32},{32,36}... | collective-permute-start | bytes 1572872 | tf_op jit(solution)/shard_map/while/body/eval_jaxpr/ppermute | solution.py:16
  275.0 1.9 copy-start.5
  278.0 1.0 copy-start.6
  279.0 10.7 %collective-permute-start = (bf16[512,512]{0,1:T(8,128)(2,1)}, bf16[512,512]{0,1:T(8,128)(2,1)S(1)}, u32[]{:S(2)}, u32[]{:S(2)}) collective-permute-start(bf16[512,512]{0,1:T(8,128)(2,1)} %get-tuple-element.290), channel_id=1, source_target_pairs={{0,4},{4,8},{8,12},{12,16},{16,20},{20,24},{24,28},{28,32},{32,36}... | collective-permute-start | bytes 1572872 | tf_op jit(solution)/shard_map/while/body/eval_jaxpr/ppermute | solution.py:16
  289.7 1.9 copy-start.5
  292.7 1.0 copy-start.6
  293.7 10.7 %collective-permute-start = (bf16[512,512]{0,1:T(8,128)(2,1)}, bf16[512,512]{0,1:T(8,128)(2,1)S(1)}, u32[]{:S(2)}, u32[]{:S(2)}) collective-permute-start(bf16[512,512]{0,1:T(8,128)(2,1)} %get-tuple-element.290), channel_id=1, source_target_pairs={{0,4},{4,8},{8,12},{12,16},{16,20},{20,24},{24,28},{28,32},{32,36}... | collective-permute-start | bytes 1572872 | tf_op jit(solution)/shard_map/while/body/eval_jaxpr/ppermute | solution.py:16
  304.4 1.9 copy-start.5
  307.4 1.0 copy-start.6
  308.4 10.7 %collective-permute-start = (bf16[512,512]{0,1:T(8,128)(2,1)}, bf16[512,512]{0,1:T(8,128)(2,1)S(1)}, u32[]{:S(2)}, u32[]{:S(2)}) collective-permute-start(bf16[512,512]{0,1:T(8,128)(2,1)} %get-tuple-element.290), channel_id=1, source_target_pairs={{0,4},{4,8},{8,12},{12,16},{16,20},{20,24},{24,28},{28,32},{32,36}... | collective-permute-start | bytes 1572872 | tf_op jit(solution)/shard_map/while/body/eval_jaxpr/ppermute | solution.py:16
  319.1 1.9 copy-start.5
  322.1 1.0 copy-start.6
Sparse Core Ops, SparseCore 0:
  9.8 63.1 all-gather.2
  325.0 164.9 all-gather.4
where the time goes:
time: 501 us; the launch traced here: 500 us
  waiting for transfers between devices  305 us (61%)
  starting transfers between devices  79.5 us (16%)
  matrix products  46.4 us (9%)
  other arithmetic  31.1 us (6%)
  local copies, waits for them, and re-layouts  22.4 us (4%)
  between operations  14.4 us (3%)
    all_gather x1, waiting for transfers between devices, body(): attended_all = lax.all_gather(attended, 'tp', axis=1, tiled=True)  158 us
    ppermute x17, waiting for transfers between devices, passed_along(): return lax.ppermute(x, axis, pairs)  95.9 us
    ppermute x17, starting transfers between devices, passed_along(): return lax.ppermute(x, axis, pairs)  73.1 us
    all_gather x1, waiting for transfers between devices, body(): gathered = lax.all_gather(residual, 'tp', axis=1, tiled=True)  50.8 us
    dot_general x17, matrix products, attend_block(): jnp.einsum('hqk,khd->qhd', weights.astype(jnp.bfloat16), key_value[:, :,...  19.7 us
    dot_general x17, matrix products, attend_block(): jnp.einsum('qhd,khd->hqk', queries, key_value[:, :, 0, :], preferred_elem...  17.8 us
    reduce_sum x17, other arithmetic, attend_block(): norm_sum = norm_sum * shrink + jnp.sum(weights, axis=2)  15.4 us
    while x90, local copies, waits for them, and re-layouts  14.6 us
  transfers between devices with their start and end apart: 20, of which 18 were waited for; matrix products, arithmetic and copies ran while one was open for 19% of the time, Pallas kernels for 0%

commit v1 on v0

--- a/solution.py
+++ b/solution.py
@@ -142,7 +142,9 @@
     pick = jnp.argmax(match.astype(jnp.int32), axis=1)
     found = jnp.any(match, axis=1)
     cache_pages = jnp.where(found[:, None, None], cand_pages[pick], jnp.zeros_like(cand_pages[:1]))
-    attended_all = lax.all_gather(attended, "tp", axis=1, tiled=True)
+    attended_all = jnp.concatenate(
+        lax.all_to_all(jnp.stack([attended] * lax.axis_size("tp")), "tp", 0, 0), axis=1
+    )
     projected = jnp.dot(attended_all, out_cols, preferred_element_type=jnp.float32)
     hidden = (residual.astype(jnp.float32) + projected).astype(jnp.bfloat16)
     return (hidden, cache_pages)

time: 501 us -> 494 us (0.986)
  the two profiles are of different devices: /device:TPU:1 before, /device:TPU:128 now
where the time goes in v1:
time: 494 us; the launch traced here: 493 us
  waiting for transfers between devices  328 us (66%)
  starting transfers between devices  54.7 us (11%)
  matrix products  45.1 us (9%)
  other arithmetic  28.9 us (6%)
  local copies, waits for them, and re-layouts  20.2 us (4%)
  between operations  14.4 us (3%)
    ppermute x17, waiting for transfers between devices, passed_along(): return lax.ppermute(x, axis, pairs)  264 us
    all_gather x1, waiting for transfers between devices, body(): gathered = lax.all_gather(residual, 'tp', axis=1, tiled=True)  54.9 us
    ppermute x17, starting transfers between devices, passed_along(): return lax.ppermute(x, axis, pairs)  32.6 us
    dot_general x17, matrix products, attend_block(): jnp.einsum('hqk,khd->qhd', weights.astype(jnp.bfloat16), key_value[:, :,...  18.9 us
    all_to_all x1, starting transfers between devices, body(): lax.all_to_all(jnp.stack([attended] * lax.axis_size('tp')), 'tp', 0, 0)  17.8 us
    dot_general x17, matrix products, attend_block(): jnp.einsum('qhd,khd->hqk', queries, key_value[:, :, 0, :], preferred_elem...  17.3 us
    reduce_sum x17, other arithmetic, attend_block(): norm_sum = norm_sum * shrink + jnp.sum(weights, axis=2)  15.4 us
    while x30, local copies, waits for them, and re-layouts  12 us
  transfers between devices with their start and end apart: 20, of which 18 were waited for; matrix products, arithmetic and copies ran while one was open for 18% of the time, Pallas kernels for 0%

profile of v1, /device:TPU:128, one launch (start us, length us, event | category | flops | bytes accessed | tf_op | source)
XLA Modules:
  0.0 492.7 jit_solution(12582836617426620356)
XLA Ops:
  7.9 1.5 copy.38
  9.4 1.3 copy.39
  10.8 4.3 all-to-all-start.1
  15.0 1.9 collective-permute-start.2
  17.7 54.9 %all-gather.2.cloned.1.call-done = bf16[512,2048]{1,0:T(8,128)(2,1)} async-done(((bf16[512,512]{1,0:T(8,128)(2,1)}), bf16[512,2048]{1,0:T(8,128)(2,1)}) %all-gather.2.cloned.1.call-update) | async-done | bytes 2097168 | tf_op jit(solution)/shard_map/all_gather | solution.py:46
  72.6 2.2 fusion.17
  74.9 2.5 fusion.67
  77.4 2.3 fusion.64
  82.5 2.1 collective-permute-start.1
  86.1 1.8 select_reduce_fusion.2
  88.0 13.5 %collective-permute-done.1 = bf16[512,512]{0,1:T(8,128)(2,1)S(1)} collective-permute-done((bf16[512,512]{0,1:T(8,128)(2,1)}, bf16[512,512]{0,1:T(8,128)(2,1)S(1)}, u32[]{:S(2)}, u32[]{:S(2)}) %collective-permute-start.1) | collective-permute-done | bytes 524320 | tf_op jit(solution)/shard_map/ppermute | solution.py:16
  101.4 1.9 select_reduce_fusion.1
  108.2 339.3 %while.20 = (s32[]{:T(128)}, bf16[512,512]{0,1:T(8,128)(2,1)}, f32[4,512]{1,0:T(4,128)S(1)}, f32[4,512]{1,0:T(4,128)S(1)}, f32[512,4,64]{0,2,1:T(8,128)S(1)}, /*...) while((s32[]{:T(128)}, bf16[512,512]{0,1:T(8,128)(2,1)}, ...), condition=%wide.region_8.9_spmd.clone, body=%wide.region_5.8_spmd.clone.sunk | while | flops 280500736 | bytes 18749628 | solution.py:126
  108.2 1.9 collective-permute-start
  110.4 16.7 %collective-permute-done = bf16[512,512]{0,1:T(8,128)(2,1)S(1)} collective-permute-done((bf16[512,512]{0,1:T(8,128)(2,1)}, bf16[512,512]{0,1:T(8,128)(2,1)S(1)}, u32[]{:S(2)}, u32[]{:S(2)}) %collective-permute-start) | collective-permute-done | bytes 524320 | tf_op jit(solution)/shard_map/while/body/eval_jaxpr/ppermute | solution.py:16
  128.9 1.1 fusion.83
  130.8 1.9 collective-permute-start
  133.0 16.7 %collective-permute-done = bf16[512,512]{0,1:T(8,128)(2,1)S(1)} collective-permute-done((bf16[512,512]{0,1:T(8,128)(2,1)}, bf16[512,512]{0,1:T(8,128)(2,1)S(1)}, u32[]{:S(2)}, u32[]{:S(2)}) %collective-permute-start) | collective-permute-done | bytes 524320 | tf_op jit(solution)/shard_map/while/body/eval_jaxpr/ppermute | solution.py:16
  151.5 1.1 fusion.83
  153.4 1.9 collective-permute-start
  155.6 16.7 %collective-permute-done = bf16[512,512]{0,1:T(8,128)(2,1)S(1)} collective-permute-done((bf16[512,512]{0,1:T(8,128)(2,1)}, bf16[512,512]{0,1:T(8,128)(2,1)S(1)}, u32[]{:S(2)}, u32[]{:S(2)}) %collective-permute-start) | collective-permute-done | bytes 524320 | tf_op jit(solution)/shard_map/while/body/eval_jaxpr/ppermute | solution.py:16
  174.1 1.1 fusion.83
  176.1 1.9 collective-permute-start
  178.2 16.7 %collective-permute-done = bf16[512,512]{0,1:T(8,128)(2,1)S(1)} collective-permute-done((bf16[512,512]{0,1:T(8,128)(2,1)}, bf16[512,512]{0,1:T(8,128)(2,1)S(1)}, u32[]{:S(2)}, u32[]{:S(2)}) %collective-permute-start) | collective-permute-done | bytes 524320 | tf_op jit(solution)/shard_map/while/body/eval_jaxpr/ppermute | solution.py:16
  196.8 1.1 fusion.83
  198.7 1.9 collective-permute-start
  200.8 16.7 %collective-permute-done = bf16[512,512]{0,1:T(8,128)(2,1)S(1)} collective-permute-done((bf16[512,512]{0,1:T(8,128)(2,1)}, bf16[512,512]{0,1:T(8,128)(2,1)S(1)}, u32[]{:S(2)}, u32[]{:S(2)}) %collective-permute-start) | collective-permute-done | bytes 524320 | tf_op jit(solution)/shard_map/while/body/eval_jaxpr/ppermute | solution.py:16
  219.4 1.1 fusion.83
  221.3 1.9 collective-permute-start
  223.5 16.7 %collective-permute-done = bf16[512,512]{0,1:T(8,128)(2,1)S(1)} collective-permute-done((bf16[512,512]{0,1:T(8,128)(2,1)}, bf16[512,512]{0,1:T(8,128)(2,1)S(1)}, u32[]{:S(2)}, u32[]{:S(2)}) %collective-permute-start) | collective-permute-done | bytes 524320 | tf_op jit(solution)/shard_map/while/body/eval_jaxpr/ppermute | solution.py:16
  242.0 1.1 fusion.83
  243.9 1.9 collective-permute-start
  246.1 16.7 %collective-permute-done = bf16[512,512]{0,1:T(8,128)(2,1)S(1)} collective-permute-done((bf16[512,512]{0,1:T(8,128)(2,1)}, bf16[512,512]{0,1:T(8,128)(2,1)S(1)}, u32[]{:S(2)}, u32[]{:S(2)}) %collective-permute-start) | collective-permute-done | bytes 524320 | tf_op jit(solution)/shard_map/while/body/eval_jaxpr/ppermute | solution.py:16
  264.6 1.1 fusion.83
  266.5 1.9 collective-permute-start
  268.7 16.7 %collective-permute-done = bf16[512,512]{0,1:T(8,128)(2,1)S(1)} collective-permute-done((bf16[512,512]{0,1:T(8,128)(2,1)}, bf16[512,512]{0,1:T(8,128)(2,1)S(1)}, u32[]{:S(2)}, u32[]{:S(2)}) %collective-permute-start) | collective-permute-done | bytes 524320 | tf_op jit(solution)/shard_map/while/body/eval_jaxpr/ppermute | solution.py:16
  287.2 1.1 fusion.83
  289.2 1.9 collective-permute-start
  291.3 16.7 %collective-permute-done = bf16[512,512]{0,1:T(8,128)(2,1)S(1)} collective-permute-done((bf16[512,512]{0,1:T(8,128)(2,1)}, bf16[512,512]{0,1:T(8,128)(2,1)S(1)}, u32[]{:S(2)}, u32[]{:S(2)}) %collective-permute-start) | collective-permute-done | bytes 524320 | tf_op jit(solution)/shard_map/while/body/eval_jaxpr/ppermute | solution.py:16
  309.9 1.1 fusion.83
  311.8 1.9 collective-permute-start
  313.9 16.7 %collective-permute-done = bf16[512,512]{0,1:T(8,128)(2,1)S(1)} collective-permute-done((bf16[512,512]{0,1:T(8,128)(2,1)}, bf16[512,512]{0,1:T(8,128)(2,1)S(1)}, u32[]{:S(2)}, u32[]{:S(2)}) %collective-permute-start) | collective-permute-done | bytes 524320 | tf_op jit(solution)/shard_map/while/body/eval_jaxpr/ppermute | solution.py:16
  332.5 1.1 fusion.83
  334.4 1.9 collective-permute-start
  336.6 16.7 %collective-permute-done = bf16[512,512]{0,1:T(8,128)(2,1)S(1)} collective-permute-done((bf16[512,512]{0,1:T(8,128)(2,1)}, bf16[512,512]{0,1:T(8,128)(2,1)S(1)}, u32[]{:S(2)}, u32[]{:S(2)}) %collective-permute-start) | collective-permute-done | bytes 524320 | tf_op jit(solution)/shard_map/while/body/eval_jaxpr/ppermute | solution.py:16
  355.1 1.1 fusion.83
  357.0 1.9 collective-permute-start
  359.2 16.7 %collective-permute-done = bf16[512,512]{0,1:T(8,128)(2,1)S(1)} collective-permute-done((bf16[512,512]{0,1:T(8,128)(2,1)}, bf16[512,512]{0,1:T(8,128)(2,1)S(1)}, u32[]{:S(2)}, u32[]{:S(2)}) %collective-permute-start) | collective-permute-done | bytes 524320 | tf_op jit(solution)/shard_map/while/body/eval_jaxpr/ppermute | solution.py:16
  377.7 1.1 fusion.83
  379.6 1.9 collective-permute-start
  381.8 16.7 %collective-permute-done = bf16[512,512]{0,1:T(8,128)(2,1)S(1)} collective-permute-done((bf16[512,512]{0,1:T(8,128)(2,1)}, bf16[512,512]{0,1:T(8,128)(2,1)S(1)}, u32[]{:S(2)}, u32[]{:S(2)}) %collective-permute-start) | collective-permute-done | bytes 524320 | tf_op jit(solution)/shard_map/while/body/eval_jaxpr/ppermute | solution.py:16
  400.3 1.1 fusion.83
  402.3 1.9 collective-permute-start
  404.4 16.7 %collective-permute-done = bf16[512,512]{0,1:T(8,128)(2,1)S(1)} collective-permute-done((bf16[512,512]{0,1:T(8,128)(2,1)}, bf16[512,512]{0,1:T(8,128)(2,1)S(1)}, u32[]{:S(2)}, u32[]{:S(2)}) %collective-permute-start) | collective-permute-done | bytes 524320 | tf_op jit(solution)/shard_map/while/body/eval_jaxpr/ppermute | solution.py:16
  423.0 1.1 fusion.83
  424.9 1.9 collective-permute-start
  427.0 16.7 %collective-permute-done = bf16[512,512]{0,1:T(8,128)(2,1)S(1)} collective-permute-done((bf16[512,512]{0,1:T(8,128)(2,1)}, bf16[512,512]{0,1:T(8,128)(2,1)S(1)}, u32[]{:S(2)}, u32[]{:S(2)}) %collective-permute-start) | collective-permute-done | bytes 524320 | tf_op jit(solution)/shard_map/while/body/eval_jaxpr/ppermute | solution.py:16
  445.6 1.1 fusion.83
  447.7 1.1 stack.3
  448.8 17.8 %all-to-all-start = ((bf16[4,512,256]{2,1,0:T(8,128)(2,1)}), bf16[4,512,256]{2,1,0:T(8,128)(2,1)}, u32[]{:S(2)}, u32[]{:S(2)}) async-start(bf16[4,512,256]{2,1,0:T(8,128)(2,1)} %stack.3), calls=%async_computation | async-start | bytes 2097152 | tf_op jit(solution)/shard_map/all_to_all | solution.py:146
  470.3 1.3 copy.42
  472.3 1.1 broadcast_select_fusion
  473.4 9.2 %all-to-all-done = bf16[4,512,256]{2,1,0:T(8,128)(2,1)} async-done(((bf16[4,512,256]{2,1,0:T(8,128)(2,1)}), bf16[4,512,256]{2,1,0:T(8,128)(2,1)}, u32[]{:S(2)}, u32[]{:S(2)}) %all-to-all-start) | async-done | bytes 1048608 | tf_op jit(solution)/shard_map/all_to_all | solution.py:146
  482.6 3.2 fusion.31
  (175 shorter events, 58.0 us)
Async XLA Ops:
  7.2 67.7 %copy-start = (bf16[2048,256]{1,0:T(8,128)(2,1)S(1)}, bf16[2048,256]{1,0:T(8,128)(2,1)}, u32[]{:S(2)}) copy-start(bf16[2048,256]{1,0:T(8,128)(2,1)} %param.14) | copy-start | bytes 3145732
  7.2 9.8 %copy-start.4 = (s32[512]{0:T(512)S(1)}, s32[512]{0:T(512)}, u32[]{:S(2)}) copy-start(s32[512]{0:T(512)} %param.18) | copy-start | bytes 6148
  7.2 9.8 %copy-start.3 = (s32[512]{0:T(512)S(1)}, s32[512]{0:T(512)}, u32[]{:S(2)}) copy-start(s32[512]{0:T(512)} %param.17) | copy-start | bytes 6148
  7.2 65.4 %all-gather.2.cloned.1.call-start = ((), (), s32[]{:S(2)}) async-start(), calls=%async_computation.2 | async-start | bytes 2621440 | tf_op jit(solution)/shard_map/all_gather | solution.py:46
  7.9 66.9 %copy-start.7 = (f32[2048]{0:T(1024)S(1)}, f32[2048]{0:T(1024)}, u32[]{:S(2)}) copy-start(f32[2048]{0:T(1024)} %param.12) | copy-start | bytes 24580
  10.8 436.9 %all-to-all-start.1 = ((bf16[256,4,512]{2,0,1:T(8,128)(2,1)}), bf16[256,4,512]{2,0,1:T(8,128)(2,1)}, u32[]{:S(2)}, u32[]{:S(2)}) async-start(bf16[256,4,512]{2,0,1:T(8,128)(2,1)} %copy.39), calls=%async_computation.1 | async-start | bytes 2097152 | tf_op jit(solution)/shard_map/all_to_all | solution.py:72
  15.0 451.6 %collective-permute-start.2 = (s32[4]{0:T(128)}, s32[4]{0:T(128)}, u32[]{:S(2)}, u32[]{:S(2)}) collective-permute-start(s32[4]{0:T(128)} %param.19), channel_id=1, source_target_pairs={{0,4},{4,8},{8,12},{12,16},{16,20},{20,24},{24,28},{28,32},{32,36}... | collective-permute-start | bytes 56 | tf_op jit(solution)/shard_map/ppermute | solution.py:16
  72.6 4.8 copy-start.1
  77.4 3.1 copy-start.6
  82.5 18.9 %collective-permute-start.1 = (bf16[512,512]{0,1:T(8,128)(2,1)}, bf16[512,512]{0,1:T(8,128)(2,1)S(1)}, u32[]{:S(2)}, u32[]{:S(2)}) collective-permute-start(bf16[512,512]{0,1:T(8,128)(2,1)} %bitcast_select_fusion), channel_id=1, source_target_pairs={{0,4},{4,8},{8,12},{12,16},{16,20},{20,24},{24,28},{28,32},{32,36}... | collective-permute-start | bytes 1572872 | tf_op jit(solution)/shard_map/ppermute | solution.py:16
  101.4 6.0 %copy-start.2 = (bf16[512,512]{0,1:T(8,128)(2,1)}, bf16[512,512]{0,1:T(8,128)(2,1)S(1)}, u32[]{:S(2)}) copy-start(bf16[512,512]{0,1:T(8,128)(2,1)S(1)} %collective-permute-done.1) | copy-start | bytes 1572868
  108.2 18.8 %collective-permute-start = (bf16[512,512]{0,1:T(8,128)(2,1)}, bf16[512,512]{0,1:T(8,128)(2,1)S(1)}, u32[]{:S(2)}, u32[]{:S(2)}) collective-permute-start(bf16[512,512]{0,1:T(8,128)(2,1)} %get-tuple-element.290), channel_id=1, source_target_pairs={{0,4},{4,8},{8,12},{12,16},{16,20},{20,24},{24,28},{28,32},{32,36}... | collective-permute-start | bytes 1572872 | tf_op jit(solution)/shard_map/while/body/eval_jaxpr/ppermute | solution.py:16
  130.8 18.8 %collective-permute-start = (bf16[512,512]{0,1:T(8,128)(2,1)}, bf16[512,512]{0,1:T(8,128)(2,1)S(1)}, u32[]{:S(2)}, u32[]{:S(2)}) collective-permute-start(bf16[512,512]{0,1:T(8,128)(2,1)} %get-tuple-element.290), channel_id=1, source_target_pairs={{0,4},{4,8},{8,12},{12,16},{16,20},{20,24},{24,28},{28,32},{32,36}... | collective-permute-start | bytes 1572872 | tf_op jit(solution)/shard_map/while/body/eval_jaxpr/ppermute | solution.py:16
  153.4 18.8 %collective-permute-start = (bf16[512,512]{0,1:T(8,128)(2,1)}, bf16[512,512]{0,1:T(8,128)(2,1)S(1)}, u32[]{:S(2)}, u32[]{:S(2)}) collective-permute-start(bf16[512,512]{0,1:T(8,128)(2,1)} %get-tuple-element.290), channel_id=1, source_target_pairs={{0,4},{4,8},{8,12},{12,16},{16,20},{20,24},{24,28},{28,32},{32,36}... | collective-permute-start | bytes 1572872 | tf_op jit(solution)/shard_map/while/body/eval_jaxpr/ppermute | solution.py:16
  176.1 18.8 %collective-permute-start = (bf16[512,512]{0,1:T(8,128)(2,1)}, bf16[512,512]{0,1:T(8,128)(2,1)S(1)}, u32[]{:S(2)}, u32[]{:S(2)}) collective-permute-start(bf16[512,512]{0,1:T(8,128)(2,1)} %get-tuple-element.290), channel_id=1, source_target_pairs={{0,4},{4,8},{8,12},{12,16},{16,20},{20,24},{24,28},{28,32},{32,36}... | collective-permute-start | bytes 1572872 | tf_op jit(solution)/shard_map/while/body/eval_jaxpr/ppermute | solution.py:16
  198.7 18.8 %collective-permute-start = (bf16[512,512]{0,1:T(8,128)(2,1)}, bf16[512,512]{0,1:T(8,128)(2,1)S(1)}, u32[]{:S(2)}, u32[]{:S(2)}) collective-permute-start(bf16[512,512]{0,1:T(8,128)(2,1)} %get-tuple-element.290), channel_id=1, source_target_pairs={{0,4},{4,8},{8,12},{12,16},{16,20},{20,24},{24,28},{28,32},{32,36}... | collective-permute-start | bytes 1572872 | tf_op jit(solution)/shard_map/while/body/eval_jaxpr/ppermute | solution.py:16
  221.3 18.8 %collective-permute-start = (bf16[512,512]{0,1:T(8,128)(2,1)}, bf16[512,512]{0,1:T(8,128)(2,1)S(1)}, u32[]{:S(2)}, u32[]{:S(2)}) collective-permute-start(bf16[512,512]{0,1:T(8,128)(2,1)} %get-tuple-element.290), channel_id=1, source_target_pairs={{0,4},{4,8},{8,12},{12,16},{16,20},{20,24},{24,28},{28,32},{32,36}... | collective-permute-start | bytes 1572872 | tf_op jit(solution)/shard_map/while/body/eval_jaxpr/ppermute | solution.py:16
  243.9 18.8 %collective-permute-start = (bf16[512,512]{0,1:T(8,128)(2,1)}, bf16[512,512]{0,1:T(8,128)(2,1)S(1)}, u32[]{:S(2)}, u32[]{:S(2)}) collective-permute-start(bf16[512,512]{0,1:T(8,128)(2,1)} %get-tuple-element.290), channel_id=1, source_target_pairs={{0,4},{4,8},{8,12},{12,16},{16,20},{20,24},{24,28},{28,32},{32,36}... | collective-permute-start | bytes 1572872 | tf_op jit(solution)/shard_map/while/body/eval_jaxpr/ppermute | solution.py:16
  266.5 18.8 %collective-permute-start = (bf16[512,512]{0,1:T(8,128)(2,1)}, bf16[512,512]{0,1:T(8,128)(2,1)S(1)}, u32[]{:S(2)}, u32[]{:S(2)}) collective-permute-start(bf16[512,512]{0,1:T(8,128)(2,1)} %get-tuple-element.290), channel_id=1, source_target_pairs={{0,4},{4,8},{8,12},{12,16},{16,20},{20,24},{24,28},{28,32},{32,36}... | collective-permute-start | bytes 1572872 | tf_op jit(solution)/shard_map/while/body/eval_jaxpr/ppermute | solution.py:16
  289.2 18.8 %collective-permute-start = (bf16[512,512]{0,1:T(8,128)(2,1)}, bf16[512,512]{0,1:T(8,128)(2,1)S(1)}, u32[]{:S(2)}, u32[]{:S(2)}) collective-permute-start(bf16[512,512]{0,1:T(8,128)(2,1)} %get-tuple-element.290), channel_id=1, source_target_pairs={{0,4},{4,8},{8,12},{12,16},{16,20},{20,24},{24,28},{28,32},{32,36}... | collective-permute-start | bytes 1572872 | tf_op jit(solution)/shard_map/while/body/eval_jaxpr/ppermute | solution.py:16
  311.8 18.8 %collective-permute-start = (bf16[512,512]{0,1:T(8,128)(2,1)}, bf16[512,512]{0,1:T(8,128)(2,1)S(1)}, u32[]{:S(2)}, u32[]{:S(2)}) collective-permute-start(bf16[512,512]{0,1:T(8,128)(2,1)} %get-tuple-element.290), channel_id=1, source_target_pairs={{0,4},{4,8},{8,12},{12,16},{16,20},{20,24},{24,28},{28,32},{32,36}... | collective-permute-start | bytes 1572872 | tf_op jit(solution)/shard_map/while/body/eval_jaxpr/ppermute | solution.py:16
  334.4 18.8 %collective-permute-start = (bf16[512,512]{0,1:T(8,128)(2,1)}, bf16[512,512]{0,1:T(8,128)(2,1)S(1)}, u32[]{:S(2)}, u32[]{:S(2)}) collective-permute-start(bf16[512,512]{0,1:T(8,128)(2,1)} %get-tuple-element.290), channel_id=1, source_target_pairs={{0,4},{4,8},{8,12},{12,16},{16,20},{20,24},{24,28},{28,32},{32,36}... | collective-permute-start | bytes 1572872 | tf_op jit(solution)/shard_map/while/body/eval_jaxpr/ppermute | solution.py:16
  357.0 18.8 %collective-permute-start = (bf16[512,512]{0,1:T(8,128)(2,1)}, bf16[512,512]{0,1:T(8,128)(2,1)S(1)}, u32[]{:S(2)}, u32[]{:S(2)}) collective-permute-start(bf16[512,512]{0,1:T(8,128)(2,1)} %get-tuple-element.290), channel_id=1, source_target_pairs={{0,4},{4,8},{8,12},{12,16},{16,20},{20,24},{24,28},{28,32},{32,36}... | collective-permute-start | bytes 1572872 | tf_op jit(solution)/shard_map/while/body/eval_jaxpr/ppermute | solution.py:16
  379.6 18.8 %collective-permute-start = (bf16[512,512]{0,1:T(8,128)(2,1)}, bf16[512,512]{0,1:T(8,128)(2,1)S(1)}, u32[]{:S(2)}, u32[]{:S(2)}) collective-permute-start(bf16[512,512]{0,1:T(8,128)(2,1)} %get-tuple-element.290), channel_id=1, source_target_pairs={{0,4},{4,8},{8,12},{12,16},{16,20},{20,24},{24,28},{28,32},{32,36}... | collective-permute-start | bytes 1572872 | tf_op jit(solution)/shard_map/while/body/eval_jaxpr/ppermute | solution.py:16
  402.3 18.8 %collective-permute-start = (bf16[512,512]{0,1:T(8,128)(2,1)}, bf16[512,512]{0,1:T(8,128)(2,1)S(1)}, u32[]{:S(2)}, u32[]{:S(2)}) collective-permute-start(bf16[512,512]{0,1:T(8,128)(2,1)} %get-tuple-element.290), channel_id=1, source_target_pairs={{0,4},{4,8},{8,12},{12,16},{16,20},{20,24},{24,28},{28,32},{32,36}... | collective-permute-start | bytes 1572872 | tf_op jit(solution)/shard_map/while/body/eval_jaxpr/ppermute | solution.py:16
  424.9 18.8 %collective-permute-start = (bf16[512,512]{0,1:T(8,128)(2,1)}, bf16[512,512]{0,1:T(8,128)(2,1)S(1)}, u32[]{:S(2)}, u32[]{:S(2)}) collective-permute-start(bf16[512,512]{0,1:T(8,128)(2,1)} %get-tuple-element.290), channel_id=1, source_target_pairs={{0,4},{4,8},{8,12},{12,16},{16,20},{20,24},{24,28},{28,32},{32,36}... | collective-permute-start | bytes 1572872 | tf_op jit(solution)/shard_map/while/body/eval_jaxpr/ppermute | solution.py:16
  447.5 22.7 %copy-start.5 = (pred[4,128]{1,0:T(4,128)(4,1)S(1)}, pred[4,128]{1,0:T(4,128)(4,1)}, u32[]{:S(2)}) copy-start(pred[4,128]{1,0:T(4,128)(4,1)} %fusion.73) | copy-start | bytes 1540
  448.8 33.8 %all-to-all-start = ((bf16[4,512,256]{2,1,0:T(8,128)(2,1)}), bf16[4,512,256]{2,1,0:T(8,128)(2,1)}, u32[]{:S(2)}, u32[]{:S(2)}) async-start(bf16[4,512,256]{2,1,0:T(8,128)(2,1)} %stack.3), calls=%async_computation | async-start | bytes 2097152 | tf_op jit(solution)/shard_map/all_to_all | solution.py:146
Sparse Core Ops, SparseCore 0:
  9.8 62.7 all-gather.1
